TPU v7x, 128 devices: a whole 4x4x4 slice. The times are simulated.
128 devices in a mesh: row: 8 (over y, core), col: 16 (over x, z).
Axes of the slice: x: 4, y: 4, z: 4, core: 2. Of those that a mesh axis runs over, the one named last changes fastest.
Arguments:
- tokens: bfloat16 [10240, 3200], P('col', 'row'), may hold values from -24 to 24
- w_qkv: bfloat16 [3200, 9600], P('row', 'col'), may hold values from -4 to 4
- q_gain: float32 [3200], replicated, may hold values from 0.5 to 1.5
- k_gain: float32 [3200], replicated, may hold values from 0.5 to 1.5
- segment_ids: int32 [8, 1280], P('row'), may hold values from 0 to 3, never falling along the last dimension, each value on 1 to 640 neighbouring positions
Outputs:
- attended: bfloat16 [10240, 3200], P(('row', 'col'))
Inputs may be any that keep to these rules, and one draw needn't show every extreme that they name: `segment_ids`: in each pack the ids never fall; each of the 4 images holds 1 to 640 tokens, one exactly 640.
All inputs are finite; a program needn't handle non-finite values.
Results may differ from a plain program's by a relative error of at most 0.033.
Values may be sent and summed in bfloat16 or wider, within the bound.
No kernel may reach another device: no remote copies, remote signals or barrier semaphores. Data moves between devices by JAX's collectives and lax.ppermute only.
A program may use at most 192 MiB of HBM per device.

v0:
```python
import jax
import jax.numpy as jnp
from jax import lax
from jax.sharding import PartitionSpec as P

ATTENTION_HEADS = 25
HEAD_WIDTH = 128
TOK_DEV = 80


def rms_norm(block, gain):
    values = block.astype(jnp.float32)
    mean_sq = jnp.mean(values * values, axis=-1, keepdims=True)
    return (values * lax.rsqrt(mean_sq + 1e-06) * gain).astype(jnp.bfloat16)


def attend(carry, queries, query_ids, keys, values, key_ids):
    best, total, accum = carry
    count_q = queries.shape[0]
    count_k = keys.shape[0]
    q3 = queries.reshape(count_q, ATTENTION_HEADS, HEAD_WIDTH)
    k3 = keys.reshape(count_k, ATTENTION_HEADS, HEAD_WIDTH)
    value_three = values.reshape(count_k, ATTENTION_HEADS, HEAD_WIDTH)
    scores = jnp.einsum(
        "qhd,khd->hqk", q3, k3, preferred_element_type=jnp.float32
    ) * HEAD_WIDTH ** (-0.5)
    mask = (query_ids[:, None] == key_ids[None, :])[None]
    masked = jnp.where(mask, scores, -1e30)
    new_best = jnp.maximum(best, jnp.max(masked, axis=-1))
    expo = jnp.where(mask, jnp.exp(masked - new_best[..., None]), 0.0)
    ratio = jnp.exp(best - new_best)
    total = total * ratio + jnp.sum(expo, axis=-1)
    weights = expo.astype(jnp.bfloat16)
    update = jnp.einsum("hqk,khd->hqd", weights, value_three, preferred_element_type=jnp.float32)
    return (new_best, total, accum * ratio[..., None] + update)


def local(tokens, w_qkv, q_gain, k_gain, segment_ids):
    width = q_gain.shape[0]
    tok_count = TOK_DEV
    position = lax.axis_index("col")
    partial_sums = jnp.dot(
        lax.all_gather(tokens, "col", axis=0, tiled=True), w_qkv, preferred_element_type=jnp.float32
    )
    summed = lax.psum_scatter(
        partial_sums.astype(jnp.bfloat16), "row", scatter_dimension=0, tiled=True
    )
    pack_ids = segment_ids[0]
    query_ids = lax.dynamic_slice_in_dim(pack_ids, position * tok_count, tok_count, 0)
    start_carry = (
        jnp.full((ATTENTION_HEADS, tok_count), -1e30, jnp.float32),
        jnp.zeros((ATTENTION_HEADS, tok_count), jnp.float32),
        jnp.zeros((ATTENTION_HEADS, tok_count, HEAD_WIDTH), jnp.float32),
    )
    whole = lax.all_gather(summed, "col", axis=1, tiled=True)
    own_rows = lax.dynamic_slice_in_dim(whole, position * tok_count, tok_count, 0)
    normed_q = rms_norm(own_rows[:, :width], q_gain)
    normed_k = rms_norm(whole[:, width : 2 * width], k_gain)
    all_values = whole[:, 2 * width :]
    block_rows = whole.shape[0] // 4
    carry = start_carry
    for block in range(4):
        lower = block * block_rows
        keys = normed_k[lower : lower + block_rows]
        key_ids = lax.dynamic_slice_in_dim(pack_ids, lower, keys.shape[0], 0)
        carry = attend(
            carry, normed_q, query_ids, keys, all_values[lower : lower + block_rows], key_ids
        )
    best, total, accum = carry
    result = accum / total[..., None]
    return jnp.transpose(result, (1, 0, 2)).reshape(tok_count, width).astype(jnp.bfloat16)


def solution(mesh):
    return jax.shard_map(
        local,
        mesh=mesh,
        in_specs=(P("col", "row"), P("row", "col"), P(), P(), P("row", None)),
        out_specs=P(("row", "col"), None),
        check_vma=False,
    )
```

profile of v0, /device:TPU:1, one launch (start us, length us, event | category | flops | bytes accessed | tf_op | source)
XLA Modules:
  0.0 368.6 jit_solution(6712530993973618767)
XLA Ops:
  6.5 0.0 copy-start
  6.5 0.0 all-gather.3.cloned.1.call-start
  6.5 0.7 all-gather.3.cloned.1.call-update
  7.3 0.0 reduce-scatter.2.cloned.1.call-start
  7.3 75.2 %all-gather.3.cloned.1.call-done = bf16[10240,400]{0,1:T(8,128)(2,1)} async-done(((bf16[640,400]{0,1:T(8,128)(2,1)}), bf16[10240,400]{0,1:T(8,128)(2,1)}) %all-gather.3.cloned.1.call-update) | async-done | bytes 8192016 | tf_op jit(solution)/shard_map/all_gather | solution.py:43
  82.6 0.0 copy-done
  82.6 11.5 %convolution_convert_fusion = bf16[10240,600]{0,1:T(8,128)(2,1)} fusion(bf16[10240,400]{0,1:T(8,128)(2,1)} %all-gather.3.cloned.1.call-done, bf16[400,600]{1,0:T(8,128)(2,1)S(1)} %copy-done), kind=kOutput, calls=%fused_computation.5 | convolution fusion | flops 4921344000 | bytes 20960000 | tf_op jit(solution)/shard_map/dot_general | solution.py:42
  94.1 0.0 copy-start.4
  94.1 0.0 reduce-scatter.2.cloned.1.call-update
  94.1 0.0 all-gather.5.cloned.1.call-start
  94.1 70.5 %reduce-scatter.2.cloned.1.call-done = bf16[1280,600]{0,1:T(8,128)(2,1)} async-done(((bf16[10240,600]{0,1:T(8,128)(2,1)}), bf16[1280,600]{0,1:T(8,128)(2,1)}) %reduce-scatter.2.cloned.1.call-update) | async-done | bytes 1536016 | tf_op jit(solution)/shard_map/reduce_scatter | solution.py:45
  164.6 0.0 all-gather.5.cloned.1.call-update
  164.6 0.0 copy-done.4
  164.6 0.1 dynamic-slice_bitcast_fusion
  164.7 0.1 slice_reduce_fusion
  164.8 0.1 broadcast_compare_fusion.1
  164.9 153.1 %all-gather.5.cloned.1.call-done = bf16[1280,9600]{0,1:T(8,128)(2,1)} async-done(((bf16[1280,600]{0,1:T(8,128)(2,1)}), bf16[1280,9600]{0,1:T(8,128)(2,1)}) %all-gather.5.cloned.1.call-update) | async-done | bytes 24576016 | tf_op jit(solution)/shard_map/all_gather | solution.py:55
  318.0 1.9 fusion.15
  320.0 0.0 copy-start.3
  320.0 5.0 %fusion = f32[1280]{0:T(1024)S(1)} fusion(bf16[1280,9600]{0,1:T(8,128)(2,1)} %all-gather.5.cloned.1.call-done), kind=kLoop, calls=%fused_computation.2 | loop fusion | flops 12286720 | bytes 8197120 | tf_op jit(solution)/shard_map/reduce_sum | solution.py:13
  325.0 0.0 copy-done.3
  325.0 5.4 %fusion.2 = bf16[1280,3200]{0,1:T(8,128)(2,1)S(1)} fusion(f32[3200]{0:T(1024)S(1)} %copy-done.3, f32[1280]{0:T(1024)S(1)} %add_rsqrt_fusion, bf16[1280,9600]{0,1:T(8,128)(2,1)} %all-gather.5.cloned.1.call-done), kind=kLoop, calls=%fused_computation.4 | loop fusion | flops 16384000 | bytes 16401920 | tf_op jit(solution)/shard_map/convert_element_type | solution.py:14
  330.4 0.0 copy-start.2
  330.4 3.3 fusion.108
  333.7 0.0 copy-done.2
  333.7 2.1 fusion.17
  335.8 0.9 fusion.6
  336.8 0.9 fusion.5
  337.7 0.9 fusion.4
  338.6 0.9 fusion.3
  339.5 2.5 fusion.11
  342.0 2.5 fusion.7
  344.6 5.7 %fusion.107 = (bf16[320,3200]{0,1:T(8,128)(2,1)S(1)}, bf16[320,3200]{0,1:T(8,128)(2,1)S(1)}, bf16[320,3200]{0,1:T(8,128)(2,1)S(1)}, bf16[320,3200]{0,1:T(8,128)(2,1)S(1)}) fusion(bf16[1280,9600]{0,1:T(8,128)(2,1)} %all-gather.5.cloned.1.call-done), kind=kLoop, calls=%fused_computation.112 | loop fusion | bytes 16384000 | tf_op jit(solution)/shard_map/slice | solution.py:67
  350.3 2.7 fusion.76
  352.9 2.9 fusion.70
  355.8 2.7 fusion.64
  358.5 0.0 copy-start.1
  358.5 2.7 fusion.81
  361.2 0.9 copy.45
  362.1 0.0 copy-done.1
  (4 shorter events, 0.1 us)
Async XLA Ops:
  6.5 76.0 %copy-start = (bf16[400,600]{1,0:T(8,128)(2,1)S(1)}, bf16[400,600]{1,0:T(8,128)(2,1)}, u32[]{:S(2)}) copy-start(bf16[400,600]{1,0:T(8,128)(2,1)} %param.6) | copy-start | bytes 1440004
  6.5 76.0 %all-gather.3.cloned.1.call-start = ((), (), s32[]{:S(2)}) async-start(), calls=%async_computation.1 | async-start | bytes 8704000 | tf_op jit(solution)/shard_map/all_gather | solution.py:43
  7.3 157.3 %reduce-scatter.2.cloned.1.call-start = ((), (), s32[]{:S(2)}) async-start(), calls=%async_computation.2 | async-start | bytes 13824000 | tf_op jit(solution)/shard_map/reduce_scatter | solution.py:45
  94.1 70.6 %copy-start.4 = (s32[1,1280]{1,0:T(1,128)S(1)}, s32[1,1280]{1,0:T(1,128)}, u32[]{:S(2)}) copy-start(s32[1,1280]{1,0:T(1,128)} %param.9) | copy-start | bytes 15364
  94.1 224.0 %all-gather.5.cloned.1.call-start = ((), (), s32[]{:S(2)}) async-start(), calls=%async_computation.3 | async-start | bytes 26112000 | tf_op jit(solution)/shard_map/all_gather | solution.py:55
  320.0 5.0 %copy-start.3 = (f32[3200]{0:T(1024)S(1)}, f32[3200]{0:T(1024)}, u32[]{:S(2)}) copy-start(f32[3200]{0:T(1024)} %param.8) | copy-start | bytes 38404
  330.4 3.3 copy-start.2
  358.5 3.6 copy-start.1
Sparse Core Ops, SparseCore 0:
  9.5 72.9 all-gather.2
  94.2 70.3 reduce-scatter.1
  166.8 151.1 all-gather.4
where the time goes:
time: 369 us
  waiting for transfers between devices  300 us (81%)
  matrix products  26.1 us (7%)
  other arithmetic  19.7 us (5%)
  between operations  13.3 us (4%)
  local copies, waits for them, and re-layouts  9.99 us (3%)
    all_gather x1, waiting for transfers between devices, local(): whole = lax.all_gather(summed, 'col', axis=1, tiled=True)  153 us
    all_gather x1, waiting for transfers between devices, local(): lax.all_gather(tokens, 'col', axis=0, tiled=True)  75.2 us
    reduce_scatter x1, waiting for transfers between devices, local(): lax.psum_scatter(partial_sums.astype(jnp.bfloat16), 'row', scatter_dimens...  70.5 us
    dot_general x1, matrix products, local(): jnp.dot(lax.all_gather(tokens, 'col', axis=0, tiled=True), w_qkv, preferr...  11.5 us
    dot_general x4, matrix products, attend(): jnp.einsum('hqk,khd->hqd', weights, value_three, preferred_element_type=j...  10.9 us
    convert_element_type x2, other arithmetic, rms_norm(): return (values * lax.rsqrt(mean_sq + 1e-06) * gain).astype(jnp.bfloat16)  7.52 us
  transfers between devices with their start and end apart: 3, of which 3 were waited for; matrix products, arithmetic and copies ran while one was open for 0% of the time, Pallas kernels for 0%

commit v1 on v0

--- a/solution.py
+++ b/solution.py
@@ -40,7 +40,11 @@
     tok_count = TOK_DEV
     position = lax.axis_index("col")
     partial_sums = jnp.dot(
-        lax.all_gather(tokens, "col", axis=0, tiled=True), w_qkv, preferred_element_type=jnp.float32
+        jnp.concatenate(
+            lax.all_to_all(jnp.stack([tokens] * lax.axis_size("col")), "col", 0, 0), axis=0
+        ),
+        w_qkv,
+        preferred_element_type=jnp.float32,
     )
     summed = lax.psum_scatter(
         partial_sums.astype(jnp.bfloat16), "row", scatter_dimension=0, tiled=True

time: 369 us -> 404 us (1.095)
  blocking collectives: 0 us -> 101 us
  waiting for transfers between devices: 300 us -> 224 us
  local copies, waits for them, and re-layouts: 9.99 us -> 19.5 us
    all_to_all x0 -> x1, blocking collectives: none -> 101 us  [local(): lax.all_to_all(jnp.stack([tokens] * lax.axis_size('col')), 'col', 0, 0)]
    all_gather x1 -> x0, waiting for transfers between devices: 75.2 us -> none  [local(): lax.all_gather(tokens, 'col', axis=0, tiled=True)]
    reshape x0 -> x1, local copies, waits for them, and re-layouts: none -> 7.78 us  [local(): jnp.concatenate(lax.all_to_all(jnp.stack([tokens] * lax.axis_size('col'))...]
  transfers between devices with their start and end apart: 3 -> 2, of which waited for: 3 -> 2; matrix products, arithmetic and copies ran while one was open for 0% -> 0% of each run, Pallas kernels for 0% -> 0%
where the time goes in v1:
time: 404 us
  waiting for transfers between devices  224 us (55%)
  blocking collectives  101 us (25%)
  matrix products  26.1 us (6%)
  other arithmetic  19.7 us (5%)
  local copies, waits for them, and re-layouts  19.5 us (5%)
  between operations  13.6 us (3%)
    all_gather x1, waiting for transfers between devices, local(): whole = lax.all_gather(summed, 'col', axis=1, tiled=True)  153 us
    all_to_all x1, blocking collectives, local(): lax.all_to_all(jnp.stack([tokens] * lax.axis_size('col')), 'col', 0, 0)  101 us
    reduce_scatter x1, waiting for transfers between devices, local(): lax.psum_scatter(partial_sums.astype(jnp.bfloat16), 'row', scatter_dimens...  70.9 us
    dot_general x1, matrix products, local(): jnp.dot(jnp.concatenate(lax.all_to_all(jnp.stack([tokens] * lax.axis_size...  11.5 us
    dot_general x4, matrix products, attend(): jnp.einsum('hqk,khd->hqd', weights, value_three, preferred_element_type=j...  10.9 us
  transfers between devices with their start and end apart: 2, of which 2 were waited for; matrix products, arithmetic and copies ran while one was open for 0% of the time, Pallas kernels for 0%

profile of v1, /device:TPU:1, one launch (start us, length us, event | category | flops | bytes accessed | tf_op | source)
XLA Modules:
  0.0 404.1 jit_solution(3491407167615124131)
XLA Ops:
  6.5 0.0 copy-start
  6.5 0.0 reduce-scatter.2.cloned.1.call-start
  6.5 1.7 stack.2
  8.3 101.3 %all_to_all.5 = bf16[16,640,400]{1,2,0:T(8,128)(2,1)} all-to-all(bf16[16,640,400]{1,2,0:T(8,128)(2,1)S(1)} %stack.2), channel_id=1, replica_groups=mesh['row'=8,'col'=16] {'col'}, dimensions={0} | all-to-all | bytes 16384000 | tf_op jit(solution)/shard_map/all_to_all | solution.py:44
  109.6 7.8 %copy.72 = bf16[16,50,8,640]{3,2,0,1:T(8,128)(2,1)} copy(bf16[16,50,8,640]{3,2,1,0:T(8,128)(2,1)} %bitcast.123) | data formatting | bytes 16384000 | tf_op jit(solution)/shard_map/reshape | solution.py:43
  117.3 0.0 copy-done
  117.3 11.5 %convolution_convert_fusion = bf16[10240,600]{0,1:T(8,128)(2,1)} fusion(bf16[10240,400]{0,1:T(8,128)(2,1)} %bitcast.132, bf16[400,600]{1,0:T(8,128)(2,1)S(1)} %copy-done), kind=kOutput, calls=%fused_computation.5 | convolution fusion | flops 4921344000 | bytes 20960000 | tf_op jit(solution)/shard_map/dot_general | solution.py:42
  128.8 0.0 copy-start.4
  128.8 0.0 reduce-scatter.2.cloned.1.call-update
  128.9 0.0 all-gather.2.cloned.1.call-start
  128.9 70.9 %reduce-scatter.2.cloned.1.call-done = bf16[1280,600]{0,1:T(8,128)(2,1)} async-done(((bf16[10240,600]{0,1:T(8,128)(2,1)}), bf16[1280,600]{0,1:T(8,128)(2,1)}) %reduce-scatter.2.cloned.1.call-update) | async-done | bytes 1536016 | tf_op jit(solution)/shard_map/reduce_scatter | solution.py:49
  199.8 0.0 all-gather.2.cloned.1.call-update
  199.9 0.0 copy-done.4
  199.9 0.1 dynamic-slice_bitcast_fusion
  199.9 0.1 slice_reduce_fusion
  200.0 0.1 broadcast_compare_fusion.1
  200.2 153.1 %all-gather.2.cloned.1.call-done = bf16[1280,9600]{0,1:T(8,128)(2,1)} async-done(((bf16[1280,600]{0,1:T(8,128)(2,1)}), bf16[1280,9600]{0,1:T(8,128)(2,1)}) %all-gather.2.cloned.1.call-update) | async-done | bytes 24576016 | tf_op jit(solution)/shard_map/all_gather | solution.py:59
  353.3 1.9 fusion.15
  355.2 0.0 copy-start.3
  355.2 5.0 %fusion = f32[1280]{0:T(1024)S(1)} fusion(bf16[1280,9600]{0,1:T(8,128)(2,1)} %all-gather.2.cloned.1.call-done), kind=kLoop, calls=%fused_computation.2 | loop fusion | flops 12286720 | bytes 8197120 | tf_op jit(solution)/shard_map/reduce_sum | solution.py:13
  360.2 0.0 copy-done.3
  360.2 5.4 %fusion.2 = bf16[1280,3200]{0,1:T(8,128)(2,1)S(1)} fusion(f32[3200]{0:T(1024)S(1)} %copy-done.3, f32[1280]{0:T(1024)S(1)} %add_rsqrt_fusion, bf16[1280,9600]{0,1:T(8,128)(2,1)} %all-gather.2.cloned.1.call-done), kind=kLoop, calls=%fused_computation.4 | loop fusion | flops 16384000 | bytes 16401920 | tf_op jit(solution)/shard_map/convert_element_type | solution.py:14
  365.6 0.0 copy-start.2
  365.6 3.3 fusion.108
  368.9 0.0 copy-done.2
  368.9 2.1 fusion.17
  371.1 0.9 fusion.6
  372.0 0.9 fusion.5
  372.9 0.9 fusion.4
  373.8 0.9 fusion.3
  374.7 2.5 fusion.11
  377.3 2.5 fusion.7
  379.8 5.7 %fusion.107 = (bf16[320,3200]{0,1:T(8,128)(2,1)S(1)}, bf16[320,3200]{0,1:T(8,128)(2,1)S(1)}, bf16[320,3200]{0,1:T(8,128)(2,1)S(1)}, bf16[320,3200]{0,1:T(8,128)(2,1)S(1)}) fusion(bf16[1280,9600]{0,1:T(8,128)(2,1)} %all-gather.2.cloned.1.call-done), kind=kLoop, calls=%fused_computation.112 | loop fusion | bytes 16384000 | tf_op jit(solution)/shard_map/slice | solution.py:71
  385.5 2.7 fusion.76
  388.2 2.9 fusion.70
  391.0 2.7 fusion.64
  393.7 0.0 copy-start.1
  393.7 2.7 fusion.81
  396.4 0.9 copy.75
  397.3 0.0 copy-done.1
  (4 shorter events, 0.1 us)
Async XLA Ops:
  6.5 110.8 %copy-start = (bf16[400,600]{1,0:T(8,128)(2,1)S(1)}, bf16[400,600]{1,0:T(8,128)(2,1)}, u32[]{:S(2)}) copy-start(bf16[400,600]{1,0:T(8,128)(2,1)} %param.6) | copy-start | bytes 1440004
  6.5 193.3 %reduce-scatter.2.cloned.1.call-start = ((), (), s32[]{:S(2)}) async-start(), calls=%async_computation.2 | async-start | bytes 13824000 | tf_op jit(solution)/shard_map/reduce_scatter | solution.py:49
  128.8 71.0 %copy-start.4 = (s32[1,1280]{1,0:T(1,128)S(1)}, s32[1,1280]{1,0:T(1,128)}, u32[]{:S(2)}) copy-start(s32[1,1280]{1,0:T(1,128)} %param.9) | copy-start | bytes 15364
  128.9 224.4 %all-gather.2.cloned.1.call-start = ((), (), s32[]{:S(2)}) async-start(), calls=%async_computation.3 | async-start | bytes 26112000 | tf_op jit(solution)/shard_map/all_gather | solution.py:59
  355.2 5.0 %copy-start.3 = (f32[3200]{0:T(1024)S(1)}, f32[3200]{0:T(1024)}, u32[]{:S(2)}) copy-start(f32[3200]{0:T(1024)} %param.8) | copy-start | bytes 38404
  365.6 3.3 copy-start.2
  393.7 3.6 copy-start.1
Sparse Core Ops, SparseCore 0:
  129.0 70.7 reduce-scatter.1
  202.0 151.1 all-gather.1
